TPU v7x, 256 devices: a whole 4x4x8 slice. The times are simulated.
256 devices in a mesh: seq: 8 (over z_lo, core), blk: 32 (over y, z_hi, x).
Axes of the slice: x: 4, y: 4, z: 8 (z_hi: 2, z_lo: 4; z = z_hi * 4 + z_lo), core: 2. Of those that a mesh axis runs over, the one named last changes fastest.
Arguments:
- stream: float32 [4096, 3072], P(('seq', 'blk')), may hold values from -39 to 39
- key_keep: int32 [4096], replicated, may hold values 0 or 1
- positions: int32 [4096, 3], replicated, may hold values from 0 to 63
- lengths: int32 [4], replicated, may hold values from 1 to 2048, 4096 in all
- step_index: int32 [4], replicated, may hold values from 0 to 27
- mod_table: bfloat16 [4, 28, 3, 3072], replicated, may hold values from -4 to 4
- w_qkv: bfloat16 [3072, 9216], P(None, 'blk'), may hold values from -0.109375 to 0.109375
- w_mlp_in: bfloat16 [3072, 12288], P(None, 'blk'), may hold values from -0.109375 to 0.109375
- q_gain: float32 [128], replicated, may hold values from 0.5 to 10
- k_gain: float32 [128], replicated, may hold values from 0.5 to 10
- w_attn_out: bfloat16 [3072, 3072], P('blk'), may hold values from -0.109375 to 0.109375
- w_mlp_out: bfloat16 [12288, 3072], P('blk'), may hold values from -0.0546875 to 0.0546875
Outputs:
- stream_next: float32 [4096, 3072], P(('seq', 'blk'))
Inputs may be any that keep to these rules, and one draw needn't show every extreme that they name: The lengths sum to 4096; the longest request has exactly 2048 tokens.
All inputs are finite; a program needn't handle non-finite values.
Results may differ from a plain program's by a relative error of at most 0.0082.
The roundings to bfloat16 on the way count: a program that leaves them out, or rounds other values in their place, can miss the bound.
Values may be sent and summed in bfloat16 or wider, within the bound.
No kernel may reach another device: no remote copies, remote signals or barrier semaphores. Data moves between devices by JAX's collectives and lax.ppermute only.
A program may use at most 64 MiB of HBM per device.

v0:
```python
import math
import jax
import jax.numpy as jnp
from jax import lax
from jax.sharding import PartitionSpec as P


def rope_table(head_size):
    first_count = head_size // 16
    second = 7 * head_size // 32
    pair_ids = jnp.arange(head_size // 2, dtype=jnp.int32)
    pair_axis = jnp.where(
        pair_ids < first_count, 0, jnp.where(pair_ids < first_count + second, 1, 2)
    )
    pair_local = jnp.where(
        pair_ids < first_count,
        pair_ids,
        jnp.where(
            pair_ids < first_count + second, pair_ids - first_count, pair_ids - first_count - second
        ),
    )
    axis_dims = jnp.where(pair_axis == 0, 2 * first_count, 2 * second)
    frequency = jnp.power(
        jnp.float32(10000.0), -(2 * pair_local).astype(jnp.float32) / axis_dims.astype(jnp.float32)
    )
    return jnp.where(
        jnp.arange(3)[:, None] == pair_axis[None, :], frequency[None, :], jnp.float32(0.0)
    )


def angles_of(places, freq_table):
    return jnp.sum(places.astype(jnp.float32)[:, :, None] * freq_table[None, :, :], axis=1)


def rotate(values, angles):
    paired = values.reshape(values.shape[:-1] + (values.shape[-1] // 2, 2))
    even_part = paired[..., 0]
    odd_part = paired[..., 1]
    cos_part = jnp.cos(angles)[:, None, :]
    sin_part = jnp.sin(angles)[:, None, :]
    turned = jnp.stack(
        [cos_part * even_part - sin_part * odd_part, sin_part * even_part + cos_part * odd_part],
        axis=-1,
    )
    return turned.reshape(values.shape)


def rms_scale(values, gain_vec):
    return values * lax.rsqrt(jnp.mean(values * values, axis=-1, keepdims=True) + 1e-06) * gain_vec


def segment_of(row_ids, request_ends):
    return jnp.sum((row_ids[:, None] >= request_ends[None, :]).astype(jnp.int32), axis=1)


def spread_rows(row_ids, query_rows, block_rows, tok_seq):
    owner = row_ids // query_rows
    within = row_ids % query_rows
    return within // block_rows * tok_seq + owner * block_rows + within % block_rows


def body(
    stream,
    key_keep,
    positions,
    lengths,
    step_index,
    mod_table,
    w_qkv,
    w_mlp_in,
    q_gain,
    k_gain,
    w_attn_out,
    w_mlp_out,
):
    blk_count = lax.axis_size("blk")
    seq_count = lax.axis_size("seq")
    seq_at = lax.axis_index("seq")
    blk_at = lax.axis_index("blk")
    block_rows = stream.shape[0]
    width = stream.shape[1]
    tok_seq = block_rows * blk_count
    head_size = q_gain.shape[0]
    local_heads = width // head_size // seq_count
    requests = mod_table.shape[0]
    step_total = mod_table.shape[1]
    inv_root = 1.0 / math.sqrt(head_size)
    request_ends = jnp.cumsum(lengths)
    own_rows = seq_at * tok_seq + blk_at * block_rows + jnp.arange(block_rows, dtype=jnp.int32)
    own_request = segment_of(own_rows, request_ends)
    step_pick = (jnp.arange(step_total, dtype=jnp.int32)[None, :] == step_index[:, None]).astype(
        jnp.bfloat16
    )
    modulation = jnp.einsum(
        "rs,rsk->rk",
        step_pick,
        mod_table.reshape(requests, step_total, 3 * width),
        preferred_element_type=jnp.float32,
    )
    member = (own_request[:, None] == jnp.arange(requests, dtype=jnp.int32)[None, :]).astype(
        jnp.float32
    )
    token_mod = jnp.dot(member, modulation, precision=lax.Precision.HIGHEST)
    mod_shift = token_mod[:, :width]
    mod_scale = token_mod[:, width : 2 * width]
    mod_gate = token_mod[:, 2 * width :]
    row_mean = jnp.mean(stream, axis=1, keepdims=True)
    centered = stream - row_mean
    row_var = jnp.mean(centered * centered, axis=1, keepdims=True)
    normed = centered * lax.rsqrt(row_var + 1e-06)
    modin = ((1.0 + mod_scale) * normed + mod_shift).astype(jnp.bfloat16)
    qkv_width = w_qkv.shape[1]
    shard_rows = lax.all_to_all(
        jnp.broadcast_to(modin[None], (blk_count,) + modin.shape), "blk", 0, 0, tiled=True
    ).reshape(blk_count * block_rows, width)
    qkv_part = jnp.dot(shard_rows, w_qkv, preferred_element_type=jnp.float32).astype(jnp.bfloat16)
    mlp_part = jax.nn.gelu(
        jnp.dot(shard_rows, w_mlp_in, preferred_element_type=jnp.float32), approximate=True
    ).astype(jnp.bfloat16)
    joined = jnp.concatenate([qkv_part, mlp_part], axis=1)
    qkv_cols = joined[:, :qkv_width]
    mlp_act = joined[:, qkv_width:]
    heads_in = lax.all_to_all(
        lax.all_to_all(qkv_cols, "blk", split_axis=0, concat_axis=1, tiled=True),
        "seq",
        split_axis=1,
        concat_axis=0,
        tiled=True,
    )
    query_rows = heads_in.shape[0]
    heads4 = heads_in.reshape(query_rows, local_heads, 3, head_size)
    query_ids = spread_rows(
        blk_at * query_rows + jnp.arange(query_rows, dtype=jnp.int32),
        query_rows,
        block_rows,
        tok_seq,
    )
    query_request = segment_of(query_ids, request_ends)
    angles = angles_of(jnp.take(positions, query_ids, axis=0), rope_table(head_size))
    query_rot = rotate(rms_scale(heads4[:, :, 0].astype(jnp.float32), q_gain), angles).astype(
        jnp.bfloat16
    )
    key_rot = rotate(rms_scale(heads4[:, :, 1].astype(jnp.float32), k_gain), angles).astype(
        jnp.bfloat16
    )
    value_rows = heads4[:, :, 2]
    run_top = jnp.full((query_rows, local_heads), -1e30, jnp.float32)
    key_part = lax.all_gather(key_rot, "blk", axis=0, tiled=True)
    value_part = lax.all_gather(value_rows, "blk", axis=0, tiled=True)
    key_ids = spread_rows(
        jnp.arange(key_part.shape[0], dtype=jnp.int32), query_rows, block_rows, tok_seq
    )
    key_request = segment_of(key_ids, request_ends)
    kept = jnp.take(key_keep, key_ids) == 1
    visible = (
        (query_request[:, None] == key_request[None, :])
        & (kept[None, :] | (query_ids[:, None] == key_ids[None, :]))
    )[:, None, :]
    scores = (
        jnp.einsum("qhd,khd->qhk", query_rot, key_part, preferred_element_type=jnp.float32)
        * inv_root
    )
    row_high = jnp.max(jnp.where(visible, scores, -1e30), axis=2)
    new_top = jnp.maximum(run_top, row_high)
    weights = jnp.where(visible, jnp.exp(scores - new_top[:, :, None]), 0.0)
    run_norm = jnp.sum(weights, axis=2)
    run_sum = jnp.einsum(
        "qhk,khd->qhd", weights.astype(jnp.bfloat16), value_part, preferred_element_type=jnp.float32
    )
    run_top, run_norm, run_sum = (new_top, run_norm, run_sum)
    attended = (run_sum / run_norm[:, :, None]).astype(jnp.bfloat16)
    attended = attended.reshape(query_rows, local_heads * head_size)
    attn_local = lax.all_to_all(
        lax.all_to_all(attended, "seq", split_axis=0, concat_axis=1, tiled=True),
        "blk",
        split_axis=1,
        concat_axis=0,
        tiled=True,
    )
    mlp_part = mlp_act
    partial = (
        jnp.dot(attn_local, w_attn_out, preferred_element_type=jnp.float32)
        + jnp.dot(mlp_part, w_mlp_out, preferred_element_type=jnp.float32)
    ).astype(jnp.bfloat16)
    pieces = lax.all_to_all(partial.reshape(blk_count, block_rows, width), "blk", 0, 0, tiled=True)
    summed = jnp.sum(pieces.astype(jnp.float32), axis=0)
    return stream + mod_gate * summed


def solution(mesh):
    in_specs = (
        P(("seq", "blk"), None),
        P(),
        P(),
        P(),
        P(),
        P(),
        P(None, "blk"),
        P(None, "blk"),
        P(),
        P(),
        P("blk", None),
        P("blk", None),
    )
    out_specs = P(("seq", "blk"), None)
    return jax.shard_map(body, mesh=mesh, in_specs=in_specs, out_specs=out_specs, check_vma=False)
```

profile of v0, /device:TPU:2, one launch (start us, length us, event | category | flops | bytes accessed | tf_op | source)
XLA Modules:
  0.0 507.3 jit_solution(7781617142355008761)
XLA Ops:
  10.6 2.8 fusion.11
  14.0 2.0 broadcast_in_dim.66
  16.0 14.3 %all-to-all-start = ((bf16[32,16,3072]{2,1,0:T(8,128)(2,1)}), bf16[32,16,3072]{2,1,0:T(8,128)(2,1)}, u32[]{:S(2)}, u32[]{:S(2)}) async-start(bf16[32,16,3072]{2,1,0:T(8,128)(2,1)} %broadcast_in_dim.66), calls=%async_computation | async-start | bytes 6291456 | tf_op jit(solution)/shard_map/all_to_all | solution.py:113
  30.3 73.6 %all-to-all-done = bf16[32,16,3072]{2,1,0:T(8,128)(2,1)} async-done(((bf16[32,16,3072]{2,1,0:T(8,128)(2,1)}), bf16[32,16,3072]{2,1,0:T(8,128)(2,1)}, u32[]{:S(2)}, u32[]{:S(2)}) %all-to-all-start) | async-done | bytes 3145760 | tf_op jit(solution)/shard_map/all_to_all | solution.py:113
  104.0 3.6 convolution_convert_fusion
  108.5 7.2 %all-to-all-start.1 = ((bf16[32,16,288]{2,1,0:T(8,128)(2,1)}), bf16[32,16,288]{2,1,0:T(8,128)(2,1)S(1)}, u32[]{:S(2)}, u32[]{:S(2)}) async-start(bf16[32,16,288]{2,1,0:T(8,128)(2,1)} %bitcast.71), calls=%async_computation.1 | async-start | bytes 786432 | tf_op jit(solution)/shard_map/all_to_all | solution.py:124
  117.2 2.8 copy.83
  120.0 2.8 gather_fusion.1
  124.4 4.0 all-to-all-done.1
  131.4 5.7 %all-to-all-start.2 = ((bf16[16,8,1152]{2,0,1:T(8,128)(2,1)}), bf16[16,8,1152]{2,0,1:T(8,128)(2,1)S(1)}, u32[]{:S(2)}, u32[]{:S(2)}) async-start(bf16[16,8,1152]{2,0,1:T(8,128)(2,1)} %copy.81), calls=%async_computation.2 | async-start | bytes 589824 | tf_op jit(solution)/shard_map/all_to_all | solution.py:123
  138.7 8.9 %all-to-all-done.2 = bf16[16,8,1152]{2,0,1:T(8,128)(2,1)S(1)} async-done(((bf16[16,8,1152]{2,0,1:T(8,128)(2,1)}), bf16[16,8,1152]{2,0,1:T(8,128)(2,1)S(1)}, u32[]{:S(2)}, u32[]{:S(2)}) %all-to-all-start.2) | async-done | bytes 294944 | tf_op jit(solution)/shard_map/all_to_all | solution.py:123
  158.4 2.0 subtract_convert_fusion
  162.6 23.0 %gather_fusion = s32[4096]{0:T(1024)S(1)} fusion(s32[4096]{0:T(1024)S(1)} %copy-done.1, s32[4096]{0:T(1024)S(1)} %broadcast_clamp_fusion), kind=kCustom, calls=%fused_computation | custom fusion | bytes 49152 | tf_op jit(solution)/shard_map/jit(_take)/gather | solution.py:154
  185.9 4.5 or_and_fusion
  190.7 67.6 %all-gather.4.cloned.1.call-done = bf16[4096,3,128]{2,0,1:T(8,128)(2,1)} async-done(((bf16[128,3,128]{2,0,1:T(8,128)(2,1)}), bf16[4096,3,128]{2,0,1:T(8,128)(2,1)}) %all-gather.4.cloned.1.call-update) | async-done | bytes 3145744 | tf_op jit(solution)/shard_map/all_gather | solution.py:148
  258.3 3.2 fusion
  261.5 2.6 copy-done.2
  265.3 106.2 %all-gather.6.cloned.1.call-done = bf16[4096,3,1,128]{0,3,1,2:T(8,128)(2,1)} async-done(((bf16[128,3,1,128]{0,3,1,2:T(8,128)(2,1)}), bf16[4096,3,1,128]{0,3,1,2:T(8,128)(2,1)}) %all-gather.6.cloned.1.call-update) | async-done | bytes 3145744 | tf_op jit(solution)/shard_map/all_gather | solution.py:149
  371.5 5.3 %fusion.23 = bf16[128,3,128]{0,2,1:T(8,128)(2,1)S(1)} fusion(f32[3,4096,128]{2,1,0:T(8,128)} %copy-done.2, f32[128,3]{0,1:T(4,128)S(1)} %broadcast_maximum_fusion, pred[128,4096]{0,1:T(8,128)(4,1)} %or_and_fusion, bf16[4096,3,1,128]{0,3,1,2:T(8,128)(2,1)} %all-gather.6.cloned.1.call-done, f32[128,3]{0,1:T(4,128)S(1)} %fusion.3), kind=kOutput, calls=%fused_computation.24 | convolution fusion | flops 407470080 | bytes 10062848 | tf_op jit(solution)/shard_map/qhk,khd->qhd/dot_general | solution.py:167
  377.1 8.7 %all_to_all.77 = bf16[8,16,384]{2,1,0:T(8,128)(2,1)S(1)} all-to-all(bf16[8,16,384]{2,1,0:T(8,128)(2,1)S(1)} %all_to_all.63), channel_id=1, replica_groups=mesh['seq'=8,'blk'=32] {'seq'}, dimensions={0} | all-to-all | bytes 196608 | tf_op jit(solution)/shard_map/all_to_all | solution.py:174
  386.0 19.6 %all_to_all.78 = bf16[16,32,96]{2,0,1:T(8,128)(2,1)S(1)} all-to-all(bf16[16,32,96]{2,0,1:T(8,128)(2,1)S(1)} %copy.98), channel_id=1, replica_groups=mesh['seq'=8,'blk'=32] {'blk'}, dimensions={1} | all-to-all | bytes 196608 | tf_op jit(solution)/shard_map/all_to_all | solution.py:173
  405.6 4.7 fusion.90
  410.3 9.6 %add_convert_fusion = bf16[512,3072]{1,0:T(8,128)(2,1)} fusion(f32[512,3072]{1,0:T(8,128)} %fusion.90, bf16[384,3072]{1,0:T(8,128)(2,1)S(1)} %copy-done, bf16[512,3072]{1,0:T(8,128)(2,1)} %bitcast.5, bf16[3072,384]{1,0:T(8,128)(2,1)} %param.19), kind=kOutput, calls=%fused_computation.8 | convolution fusion | flops 2420834304 | bytes 17301504 | tf_op jit(solution)/shard_map/dot_general | solution.py:183
  419.9 79.4 %all_to_all.79 = bf16[32,16,3072]{2,1,0:T(8,128)(2,1)S(1)} all-to-all(bf16[32,16,3072]{2,1,0:T(8,128)(2,1)} %bitcast.68), channel_id=1, replica_groups=mesh['seq'=8,'blk'=32] {'blk'}, dimensions={0} | all-to-all | bytes 6291456 | tf_op jit(solution)/shard_map/all_to_all | solution.py:185
  (85 shorter events, 29.3 us)
Async XLA Ops:
  6.5 403.8 %copy-start = (bf16[384,3072]{1,0:T(8,128)(2,1)S(1)}, bf16[384,3072]{1,0:T(8,128)(2,1)}, u32[]{:S(2)}) copy-start(bf16[384,3072]{1,0:T(8,128)(2,1)} %param.23) | copy-start | bytes 7077892
  6.5 7.3 %copy-start.3 = (f32[16,3072]{1,0:T(8,128)S(1)}, f32[16,3072]{1,0:T(8,128)}, u32[]{:S(2)}) copy-start(f32[16,3072]{1,0:T(8,128)} %param.12) | copy-start | bytes 589828
  10.5 5.5 %copy-start.11 = (s32[4,1]{0,1:T(1,128)}, s32[4,1]{0,1:T(1,128)S(1)}, u32[]{:S(2)}) copy-start(s32[4,1]{0,1:T(1,128)S(1)} %reduce-window.8) | copy-start | bytes 52
  16.0 87.9 %all-to-all-start = ((bf16[32,16,3072]{2,1,0:T(8,128)(2,1)}), bf16[32,16,3072]{2,1,0:T(8,128)(2,1)}, u32[]{:S(2)}, u32[]{:S(2)}) async-start(bf16[32,16,3072]{2,1,0:T(8,128)(2,1)} %broadcast_in_dim.66), calls=%async_computation | async-start | bytes 6291456 | tf_op jit(solution)/shard_map/all_to_all | solution.py:113
  103.9 11.8 %copy-start.9 = (f32[128]{0:T(128)S(1)}, f32[128]{0:T(128)}, u32[]{:S(2)}) copy-start(f32[128]{0:T(128)} %param.21) | copy-start | bytes 1540
  104.0 12.5 %copy-start.10 = (f32[128]{0:T(128)S(1)}, f32[128]{0:T(128)}, u32[]{:S(2)}) copy-start(f32[128]{0:T(128)} %param.20) | copy-start | bytes 1540
  108.5 19.9 %all-to-all-start.1 = ((bf16[32,16,288]{2,1,0:T(8,128)(2,1)}), bf16[32,16,288]{2,1,0:T(8,128)(2,1)S(1)}, u32[]{:S(2)}, u32[]{:S(2)}) async-start(bf16[32,16,288]{2,1,0:T(8,128)(2,1)} %bitcast.71), calls=%async_computation.1 | async-start | bytes 786432 | tf_op jit(solution)/shard_map/all_to_all | solution.py:124
  131.4 16.2 %all-to-all-start.2 = ((bf16[16,8,1152]{2,0,1:T(8,128)(2,1)}), bf16[16,8,1152]{2,0,1:T(8,128)(2,1)S(1)}, u32[]{:S(2)}, u32[]{:S(2)}) async-start(bf16[16,8,1152]{2,0,1:T(8,128)(2,1)} %copy.81), calls=%async_computation.2 | async-start | bytes 589824 | tf_op jit(solution)/shard_map/all_to_all | solution.py:123
  137.1 121.1 %all-gather.4.cloned.1.call-start = ((), (), s32[]{:S(2)}) async-start(), calls=%async_computation.6 | async-start | bytes 3244032 | tf_op jit(solution)/shard_map/all_gather | solution.py:148
  147.5 0.7 copy-start.5
  148.2 14.3 %copy-start.1 = (s32[4096]{0:T(1024)S(1)}, s32[4096]{0:T(1024)}, u32[]{:S(2)}) copy-start(s32[4096]{0:T(1024)} %param.13) | copy-start | bytes 49156
  150.4 11.2 %copy-start.6 = (bf16[128,3,1,128]{3,2,1,0:T(2,128)(2,1)S(1)}, bf16[128,3,1,128]{3,2,1,0:T(2,128)(2,1)}, u32[]{:S(2)}) copy-start(bf16[128,3,1,128]{3,2,1,0:T(2,128)(2,1)} %get-tuple-element.5) | copy-start | bytes 294916
  161.4 210.2 %all-gather.6.cloned.1.call-start = ((), (), s32[]{:S(2)}) async-start(), calls=%async_computation.7 | async-start | bytes 3244032 | tf_op jit(solution)/shard_map/all_gather | solution.py:149
  162.5 23.1 %copy-start.12 = (s32[4,1]{0,1:T(1,128)S(1)}, s32[4,1]{0,1:T(1,128)}, u32[]{:S(2)}) copy-start(s32[4,1]{0,1:T(1,128)} %copy-done.11) | copy-start | bytes 52
  162.5 27.9 %copy-start.7 = (bf16[128,3,64,1]{0,3,2,1:T(2,128)(2,1)S(1)}, bf16[128,3,64,1]{0,3,2,1:T(2,128)(2,1)}, u32[]{:S(2)}) copy-start(bf16[128,3,64,1]{0,3,2,1:T(2,128)(2,1)} %get-tuple-element.8) | copy-start | bytes 147460
  162.5 27.9 %copy-start.8 = (bf16[128,3,64,1]{0,3,2,1:T(2,128)(2,1)S(1)}, bf16[128,3,64,1]{0,3,2,1:T(2,128)(2,1)}, u32[]{:S(2)}) copy-start(bf16[128,3,64,1]{0,3,2,1:T(2,128)(2,1)} %get-tuple-element.9) | copy-start | bytes 147460
  258.3 5.9 %copy-start.4 = (pred[128,4096]{0,1:T(8,128)(4,1)S(1)}, pred[128,4096]{0,1:T(8,128)(4,1)}, u32[]{:S(2)}) copy-start(pred[128,4096]{0,1:T(8,128)(4,1)} %or_and_fusion) | copy-start | bytes 1572868
  261.4 2.7 copy-start.2
Sparse Core Ops, SparseCore 0:
  161.5 96.7 all-gather.3
  261.5 110.0 all-gather.5
where the time goes:
time: 508 us; the launch traced here: 507 us
  waiting for transfers between devices  260 us (51%)
  blocking collectives  108 us (21%)
  local copies, waits for them, and re-layouts  47.8 us (9%)
  matrix products  29.6 us (6%)
  starting transfers between devices  27.5 us (5%)
  other arithmetic  20.6 us (4%)
  between operations  13.7 us (3%)
    all_gather x1, waiting for transfers between devices, body(): value_part = lax.all_gather(value_rows, 'blk', axis=0, tiled=True)  106 us
    all_to_all x1, blocking collectives, body(): lax.all_to_all(partial.reshape(blk_count, block_rows, width), 'blk', 0, 0...  79.4 us
    all_to_all x1, waiting for transfers between devices, body(): lax.all_to_all(jnp.broadcast_to(modin[None], (blk_count,) + modin.shape),...  73.6 us
    all_gather x1, waiting for transfers between devices, body(): key_part = lax.all_gather(key_rot, 'blk', axis=0, tiled=True)  67.6 us
    gather x1, local copies, waits for them, and re-layouts, body(): kept = jnp.take(key_keep, key_ids) == 1  23 us
    all_to_all x1, blocking collectives, body(): lax.all_to_all(lax.all_to_all(attended, 'seq', split_axis=0, concat_axis=...  19.6 us
    all_to_all x1, starting transfers between devices, body(): lax.all_to_all(jnp.broadcast_to(modin[None], (blk_count,) + modin.shape),...  14.3 us
  transfers between devices with their start and end apart: 5, of which 5 were waited for; matrix products, arithmetic and copies ran while one was open for 9% of the time, Pallas kernels for 0%

commit v1 on v0

--- a/solution.py
+++ b/solution.py
@@ -145,7 +145,10 @@
     )
     value_rows = heads4[:, :, 2]
     run_top = jnp.full((query_rows, local_heads), -1e30, jnp.float32)
-    key_part = lax.all_gather(key_rot, "blk", axis=0, tiled=True)
+    key_part = jnp.concatenate(
+        lax.all_to_all(jnp.stack([key_rot for _ in range(lax.axis_size("blk"))]), "blk", 0, 0),
+        axis=0,
+    )
     value_part = lax.all_gather(value_rows, "blk", axis=0, tiled=True)
     key_ids = spread_rows(
         jnp.arange(key_part.shape[0], dtype=jnp.int32), query_rows, block_rows, tok_seq

time: 508 us -> 452 us (0.89)
  waiting for transfers between devices: 260 us -> 197 us
  starting transfers between devices: 27.5 us -> 35.5 us
    all_gather x1 -> x0, waiting for transfers between devices: 67.6 us -> none  [body(): key_part = lax.all_gather(key_rot, 'blk', axis=0, tiled=True)]
    all_to_all x0 -> x1, waiting for transfers between devices: none -> 49.2 us  [body(): lax.all_to_all(jnp.stack([key_rot for _ in range(lax.axis_size('blk'))]),...]
    all_gather x1, waiting for transfers between devices: 106 us -> 61.4 us  [body(): value_part = lax.all_gather(value_rows, 'blk', axis=0, tiled=True)]
    all_to_all x0 -> x1, starting transfers between devices: none -> 8.01 us  [body(): lax.all_to_all(jnp.stack([key_rot for _ in range(lax.axis_size('blk'))]),...]
  transfers between devices with their start and end apart: 5 -> 5, of which waited for: 5 -> 5; matrix products, arithmetic and copies ran while one was open for 9% -> 10% of each run, Pallas kernels for 0% -> 0%
where the time goes in v1:
time: 452 us; the launch traced here: 451 us
  waiting for transfers between devices  197 us (44%)
  blocking collectives  108 us (24%)
  local copies, waits for them, and re-layouts  51.4 us (11%)
  starting transfers between devices  35.5 us (8%)
  matrix products  27.6 us (6%)
  other arithmetic  18 us (4%)
  between operations  13.7 us (3%)
    all_to_all x1, blocking collectives, body(): lax.all_to_all(partial.reshape(blk_count, block_rows, width), 'blk', 0, 0...  79.4 us
    all_to_all x1, waiting for transfers between devices, body(): lax.all_to_all(jnp.broadcast_to(modin[None], (blk_count,) + modin.shape),...  73.6 us
    all_gather x1, waiting for transfers between devices, body(): value_part = lax.all_gather(value_rows, 'blk', axis=0, tiled=True)  61.4 us
    all_to_all x1, waiting for transfers between devices, body(): lax.all_to_all(jnp.stack([key_rot for _ in range(lax.axis_size('blk'))]),...  49.2 us
    gather x1, local copies, waits for them, and re-layouts, body(): kept = jnp.take(key_keep, key_ids) == 1  23 us
    all_to_all x1, blocking collectives, body(): lax.all_to_all(lax.all_to_all(attended, 'seq', split_axis=0, concat_axis=...  19.6 us
    all_to_all x1, starting transfers between devices, body(): lax.all_to_all(jnp.broadcast_to(modin[None], (blk_count,) + modin.shape),...  14.3 us
    dot_general x1, matrix products, body(): jnp.dot(mlp_part, w_mlp_out, preferred_element_type=jnp.float32)  9.59 us
  transfers between devices with their start and end apart: 5, of which 5 were waited for; matrix products, arithmetic and copies ran while one was open for 10% of the time, Pallas kernels for 0%

profile of v1, /device:TPU:2, one launch (start us, length us, event | category | flops | bytes accessed | tf_op | source)
XLA Modules:
  0.0 451.0 jit_solution(16291574892750711570)
XLA Ops:
  10.6 2.8 fusion.11
  16.0 14.3 %all-to-all-start = ((bf16[32,16,3072]{2,1,0:T(8,128)(2,1)}), bf16[32,16,3072]{2,1,0:T(8,128)(2,1)}, u32[]{:S(2)}, u32[]{:S(2)}) async-start(bf16[32,16,3072]{2,1,0:T(8,128)(2,1)} %broadcast_in_dim.66), calls=%async_computation | async-start | bytes 6291456 | tf_op jit(solution)/shard_map/all_to_all | solution.py:113
  30.3 73.6 %all-to-all-done = bf16[32,16,3072]{2,1,0:T(8,128)(2,1)} async-done(((bf16[32,16,3072]{2,1,0:T(8,128)(2,1)}), bf16[32,16,3072]{2,1,0:T(8,128)(2,1)}, u32[]{:S(2)}, u32[]{:S(2)}) %all-to-all-start) | async-done | bytes 3145760 | tf_op jit(solution)/shard_map/all_to_all | solution.py:113
  104.0 3.6 convolution_convert_fusion
  108.5 7.2 %all-to-all-start.1 = ((bf16[32,16,288]{2,1,0:T(8,128)(2,1)}), bf16[32,16,288]{2,1,0:T(8,128)(2,1)S(1)}, u32[]{:S(2)}, u32[]{:S(2)}) async-start(bf16[32,16,288]{2,1,0:T(8,128)(2,1)} %bitcast.73), calls=%async_computation.1 | async-start | bytes 786432 | tf_op jit(solution)/shard_map/all_to_all | solution.py:124
  117.2 2.8 copy.85
  120.0 2.8 gather_fusion.1
  124.4 4.0 all-to-all-done.1
  131.4 5.7 %all-to-all-start.2 = ((bf16[16,8,1152]{2,0,1:T(8,128)(2,1)}), bf16[16,8,1152]{2,0,1:T(8,128)(2,1)S(1)}, u32[]{:S(2)}, u32[]{:S(2)}) async-start(bf16[16,8,1152]{2,0,1:T(8,128)(2,1)} %copy.83), calls=%async_computation.2 | async-start | bytes 589824 | tf_op jit(solution)/shard_map/all_to_all | solution.py:123
  138.6 8.9 %all-to-all-done.2 = bf16[16,8,1152]{2,0,1:T(8,128)(2,1)S(1)} async-done(((bf16[16,8,1152]{2,0,1:T(8,128)(2,1)}), bf16[16,8,1152]{2,0,1:T(8,128)(2,1)S(1)}, u32[]{:S(2)}, u32[]{:S(2)}) %all-to-all-start.2) | async-done | bytes 294944 | tf_op jit(solution)/shard_map/all_to_all | solution.py:123
  157.4 2.5 stack.9
  159.9 8.0 %all-to-all-start.3 = ((bf16[32,128,3,128]{3,1,2,0:T(8,128)(2,1)}), bf16[32,128,3,128]{3,1,2,0:T(8,128)(2,1)}, u32[]{:S(2)}, u32[]{:S(2)}) async-start(bf16[32,128,3,128]{3,1,2,0:T(8,128)(2,1)} %stack.9), calls=%async_computation.3 | async-start | bytes 6291456 | tf_op jit(solution)/shard_map/all_to_all | solution.py:149
  169.1 23.0 %gather_fusion = s32[4096]{0:T(1024)S(1)} fusion(s32[4096]{0:T(1024)S(1)} %copy-done.1, s32[4096]{0:T(1024)S(1)} %broadcast_clamp_fusion), kind=kCustom, calls=%fused_computation | custom fusion | bytes 49152 | tf_op jit(solution)/shard_map/jit(_take)/gather | solution.py:157
  192.5 4.5 %or_and_fusion = pred[128,4096]{0,1:T(8,128)(4,1)} fusion(s32[128]{0:T(128)S(1)} %fusion.72, s32[128]{0:T(128)S(1)} %convert_reduce_fusion.2, s32[4096]{0:T(1024)S(1)} %fusion.56, s32[4096]{0:T(1024)S(1)} %convert_reduce_fusion.1, pred[4096]{0:T(1024)(128)(4,1)S(1)} %select_compare_fusion), kind=kLoop, calls=%fused_computation.19 | loop fusion | flops 2097152 | bytes 562176 | tf_op jit(solution)/shard_map/and | solution.py:159
  197.2 49.2 %all-to-all-done.3 = bf16[32,128,3,128]{3,1,2,0:T(8,128)(2,1)} async-done(((bf16[32,128,3,128]{3,1,2,0:T(8,128)(2,1)}), bf16[32,128,3,128]{3,1,2,0:T(8,128)(2,1)}, u32[]{:S(2)}, u32[]{:S(2)}) %all-to-all-start.3) | async-done | bytes 3145760 | tf_op jit(solution)/shard_map/all_to_all | solution.py:149
  246.4 2.3 copy.92
  250.0 2.6 copy-done.2
  253.8 61.4 %all-gather.3.cloned.1.call-done = bf16[4096,3,1,128]{0,3,1,2:T(8,128)(2,1)} async-done(((bf16[128,3,1,128]{0,3,1,2:T(8,128)(2,1)}), bf16[4096,3,1,128]{0,3,1,2:T(8,128)(2,1)}) %all-gather.3.cloned.1.call-update) | async-done | bytes 3145744 | tf_op jit(solution)/shard_map/all_gather | solution.py:152
  315.2 5.3 %fusion.23 = bf16[128,3,128]{0,2,1:T(8,128)(2,1)S(1)} fusion(f32[3,4096,128]{2,1,0:T(8,128)} %copy-done.2, f32[128,3]{0,1:T(4,128)S(1)} %broadcast_maximum_fusion, pred[128,4096]{0,1:T(8,128)(4,1)} %or_and_fusion, bf16[4096,3,1,128]{0,3,1,2:T(8,128)(2,1)} %all-gather.3.cloned.1.call-done, f32[128,3]{0,1:T(4,128)S(1)} %fusion.3), kind=kOutput, calls=%fused_computation.24 | convolution fusion | flops 407470080 | bytes 10062848 | tf_op jit(solution)/shard_map/qhk,khd->qhd/dot_general | solution.py:170
  320.8 8.7 %all_to_all.82 = bf16[8,16,384]{2,1,0:T(8,128)(2,1)S(1)} all-to-all(bf16[8,16,384]{2,1,0:T(8,128)(2,1)S(1)} %all_to_all.67), channel_id=1, replica_groups=mesh['seq'=8,'blk'=32] {'seq'}, dimensions={0} | all-to-all | bytes 196608 | tf_op jit(solution)/shard_map/all_to_all | solution.py:177
  329.7 19.6 %all_to_all.83 = bf16[16,32,96]{2,0,1:T(8,128)(2,1)S(1)} all-to-all(bf16[16,32,96]{2,0,1:T(8,128)(2,1)S(1)} %copy.101), channel_id=1, replica_groups=mesh['seq'=8,'blk'=32] {'blk'}, dimensions={1} | all-to-all | bytes 196608 | tf_op jit(solution)/shard_map/all_to_all | solution.py:176
  349.3 4.7 %fusion.90 = f32[512,3072]{1,0:T(8,128)} fusion(bf16[512,96]{1,0:T(8,128)(2,1)S(1)} %bitcast.75, bf16[96,3072]{1,0:T(8,128)(2,1)} %param.22), kind=kOutput, calls=%fused_computation.169 | convolution fusion | flops 301989888 | bytes 6979584 | tf_op jit(solution)/shard_map/dot_general | solution.py:185
  354.0 9.6 %add_convert_fusion = bf16[512,3072]{1,0:T(8,128)(2,1)} fusion(f32[512,3072]{1,0:T(8,128)} %fusion.90, bf16[384,3072]{1,0:T(8,128)(2,1)S(1)} %copy-done, bf16[512,3072]{1,0:T(8,128)(2,1)} %bitcast.5, bf16[3072,384]{1,0:T(8,128)(2,1)} %param.19), kind=kOutput, calls=%fused_computation.8 | convolution fusion | flops 2420834304 | bytes 17301504 | tf_op jit(solution)/shard_map/dot_general | solution.py:186
  363.6 79.4 %all_to_all.84 = bf16[32,16,3072]{2,1,0:T(8,128)(2,1)S(1)} all-to-all(bf16[32,16,3072]{2,1,0:T(8,128)(2,1)} %bitcast.70), channel_id=1, replica_groups=mesh['seq'=8,'blk'=32] {'blk'}, dimensions={0} | all-to-all | bytes 6291456 | tf_op jit(solution)/shard_map/all_to_all | solution.py:188
  (86 shorter events, 30.5 us)
Async XLA Ops:
  6.5 347.4 %copy-start = (bf16[384,3072]{1,0:T(8,128)(2,1)S(1)}, bf16[384,3072]{1,0:T(8,128)(2,1)}, u32[]{:S(2)}) copy-start(bf16[384,3072]{1,0:T(8,128)(2,1)} %param.23) | copy-start | bytes 7077892
  6.5 7.3 %copy-start.3 = (f32[16,3072]{1,0:T(8,128)S(1)}, f32[16,3072]{1,0:T(8,128)}, u32[]{:S(2)}) copy-start(f32[16,3072]{1,0:T(8,128)} %param.12) | copy-start | bytes 589828
  10.5 5.5 %copy-start.11 = (s32[4,1]{0,1:T(1,128)}, s32[4,1]{0,1:T(1,128)S(1)}, u32[]{:S(2)}) copy-start(s32[4,1]{0,1:T(1,128)S(1)} %reduce-window.8) | copy-start | bytes 52
  16.0 87.9 %all-to-all-start = ((bf16[32,16,3072]{2,1,0:T(8,128)(2,1)}), bf16[32,16,3072]{2,1,0:T(8,128)(2,1)}, u32[]{:S(2)}, u32[]{:S(2)}) async-start(bf16[32,16,3072]{2,1,0:T(8,128)(2,1)} %broadcast_in_dim.66), calls=%async_computation | async-start | bytes 6291456 | tf_op jit(solution)/shard_map/all_to_all | solution.py:113
  103.9 11.8 %copy-start.9 = (f32[128]{0:T(128)S(1)}, f32[128]{0:T(128)}, u32[]{:S(2)}) copy-start(f32[128]{0:T(128)} %param.21) | copy-start | bytes 1540
  104.0 12.5 %copy-start.10 = (f32[128]{0:T(128)S(1)}, f32[128]{0:T(128)}, u32[]{:S(2)}) copy-start(f32[128]{0:T(128)} %param.20) | copy-start | bytes 1540
  108.5 19.9 %all-to-all-start.1 = ((bf16[32,16,288]{2,1,0:T(8,128)(2,1)}), bf16[32,16,288]{2,1,0:T(8,128)(2,1)S(1)}, u32[]{:S(2)}, u32[]{:S(2)}) async-start(bf16[32,16,288]{2,1,0:T(8,128)(2,1)} %bitcast.73), calls=%async_computation.1 | async-start | bytes 786432 | tf_op jit(solution)/shard_map/all_to_all | solution.py:124
  131.4 16.2 %all-to-all-start.2 = ((bf16[16,8,1152]{2,0,1:T(8,128)(2,1)}), bf16[16,8,1152]{2,0,1:T(8,128)(2,1)S(1)}, u32[]{:S(2)}, u32[]{:S(2)}) async-start(bf16[16,8,1152]{2,0,1:T(8,128)(2,1)} %copy.83), calls=%async_computation.2 | async-start | bytes 589824 | tf_op jit(solution)/shard_map/all_to_all | solution.py:123
  147.5 0.7 copy-start.5
  159.9 8.2 %copy-start.6 = (bf16[128,3,1,128]{3,2,1,0:T(2,128)(2,1)S(1)}, bf16[128,3,1,128]{3,2,1,0:T(2,128)(2,1)}, u32[]{:S(2)}) copy-start(bf16[128,3,1,128]{3,2,1,0:T(2,128)(2,1)} %get-tuple-element.5) | copy-start | bytes 294916
  159.9 9.2 %copy-start.1 = (s32[4096]{0:T(1024)S(1)}, s32[4096]{0:T(1024)}, u32[]{:S(2)}) copy-start(s32[4096]{0:T(1024)} %param.13) | copy-start | bytes 49156
  159.9 86.5 %all-to-all-start.3 = ((bf16[32,128,3,128]{3,1,2,0:T(8,128)(2,1)}), bf16[32,128,3,128]{3,1,2,0:T(8,128)(2,1)}, u32[]{:S(2)}, u32[]{:S(2)}) async-start(bf16[32,128,3,128]{3,1,2,0:T(8,128)(2,1)} %stack.9), calls=%async_computation.3 | async-start | bytes 6291456 | tf_op jit(solution)/shard_map/all_to_all | solution.py:149
  167.9 147.2 %all-gather.3.cloned.1.call-start = ((), (), s32[]{:S(2)}) async-start(), calls=%async_computation.7 | async-start | bytes 3244032 | tf_op jit(solution)/shard_map/all_gather | solution.py:152
  169.1 23.1 %copy-start.12 = (s32[4,1]{0,1:T(1,128)S(1)}, s32[4,1]{0,1:T(1,128)}, u32[]{:S(2)}) copy-start(s32[4,1]{0,1:T(1,128)} %copy-done.11) | copy-start | bytes 52
  169.1 27.9 %copy-start.7 = (bf16[128,3,64,1]{0,3,2,1:T(2,128)(2,1)S(1)}, bf16[128,3,64,1]{0,3,2,1:T(2,128)(2,1)}, u32[]{:S(2)}) copy-start(bf16[128,3,64,1]{0,3,2,1:T(2,128)(2,1)} %get-tuple-element.8) | copy-start | bytes 147460
  169.1 27.9 %copy-start.8 = (bf16[128,3,64,1]{0,3,2,1:T(2,128)(2,1)S(1)}, bf16[128,3,64,1]{0,3,2,1:T(2,128)(2,1)}, u32[]{:S(2)}) copy-start(bf16[128,3,64,1]{0,3,2,1:T(2,128)(2,1)} %get-tuple-element.9) | copy-start | bytes 147460
  246.4 2.4 copy-start.4
  250.0 2.7 copy-start.2
Sparse Core Ops, SparseCore 0:
  172.0 143.1 all-gather.2
